TPU v7x, 128 devices: a whole 4x4x4 slice. The times are simulated.
128 devices in a mesh: dp: 2 (over core), seq: 16 (over z, x), head: 4 (over y).
Axes of the slice: x: 4, y: 4, z: 4, core: 2. Of those that a mesh axis runs over, the one named last changes fastest.
Arguments:
- queries: bfloat16 [2, 10240, 2048], P('dp', ('seq', 'head')), may hold values from -45 to 45
- key_rows: bfloat16 [2, 10240, 2048], P('dp', ('seq', 'head')), may hold values from -6 to 6
- values: bfloat16 [2, 10240, 2048], P('dp', ('seq', 'head')), may hold values from -6 to 6
- rand_blocks: int32 [160, 16, 4], P('seq', 'head'), may hold values from 0 to 159, as said below
- out_weight: bfloat16 [2048, 2048], P('head'), may hold values from -0.125 to 0.125
- cotangent: bfloat16 [2, 10240, 2048], P('dp', ('seq', 'head')), may hold values from -6 to 6
Outputs:
- layer_out: bfloat16 [2, 10240, 2048], P('dp', ('seq', 'head'))
- grad_queries: bfloat16 [2, 10240, 2048], P('dp', ('seq', 'head'))
- grad_keys: bfloat16 [2, 10240, 2048], P('dp', ('seq', 'head'))
- grad_values: bfloat16 [2, 10240, 2048], P('dp', ('seq', 'head'))
- weight_grad: float32 [2048, 2048], P('head')
Inputs may be any that keep to these rules, and one draw needn't show every extreme that they name: `rand_blocks`: key block b lies in range b // 10 of seq. Over the 10 query blocks of one index of seq and the 4 heads of one index of head, at most 15 of the listed random blocks lie in any one range of seq; in every draw, for every index of head, some range of seq receives exactly 15 of them from every index of seq.
All inputs are finite; a program needn't handle non-finite values.
Results may differ from a plain program's by a relative error of at most 0.034.
Values may be sent and summed in bfloat16 or wider, within the bound.
No kernel may reach another device: no remote copies, remote signals or barrier semaphores. Data moves between devices by JAX's collectives and lax.ppermute only.
A program may use at most 192 MiB of HBM per device.

v0:
```python
import math
import jax
import jax.numpy as jnp
from jax import lax
from jax.sharding import PartitionSpec as P

HEAD_SIZE = 128
BLOCK_TOKENS = 64


def with_halo(block, sides, width):
    for axis, dim in sides:
        count = lax.axis_size(axis)
        forward = [(i, i + 1) for i in range(count - 1)]
        backward = [(target, source) for source, target in forward]
        low = lax.ppermute(
            lax.slice_in_dim(block, block.shape[dim] - width, None, axis=dim), axis, forward
        )
        high = lax.ppermute(lax.slice_in_dim(block, 0, width, axis=dim), axis, backward)
        block = jnp.concatenate([low, block, high], axis=dim)
    return block


def from_root(block, axis, holder):
    block = jnp.where(lax.axis_index(axis) == holder, block, jnp.zeros_like(block))
    return lax.psum(block, axis)


def per_device(queries, key_rows, values, rand_blocks, out_weight, cotangent):
    block_len = BLOCK_TOKENS
    head_dim = HEAD_SIZE
    seq_count = lax.axis_size("seq")
    seq_index = lax.axis_index("seq")
    q_heads, k_heads, v_heads = (
        lax.all_to_all(queries, "head", split_axis=2, concat_axis=1, tiled=True),
        lax.all_to_all(key_rows, "head", split_axis=2, concat_axis=1, tiled=True),
        lax.all_to_all(values, "head", split_axis=2, concat_axis=1, tiled=True),
    )
    q_rows = q_heads[0]
    shard_len = q_rows.shape[0]
    width_cols = q_rows.shape[1]
    head_count = width_cols // head_dim
    block_count = shard_len // block_len
    rand_count = rand_blocks.shape[2]
    key_value = jnp.concatenate([k_heads[0], v_heads[0]], axis=1)
    padded = with_halo(key_value, (("seq", 0),), block_len)
    first_block = from_root(key_value[:block_len], "seq", 0)
    requests = jnp.transpose(rand_blocks, (0, 2, 1)).reshape(-1)
    request_count = requests.shape[0]
    head_of = jnp.arange(request_count, dtype=jnp.int32) % head_count
    capacity = 3 * request_count // (2 * seq_count)
    owners = requests // block_count
    offsets = requests % block_count
    one_hot = (owners[:, None] == jnp.arange(seq_count, dtype=jnp.int32)[None, :]).astype(jnp.int32)
    position = jnp.sum(one_hot * (jnp.cumsum(one_hot, axis=0) - 1), axis=1)
    slot_of = owners * capacity + position
    asked_codes = (
        jnp.full((seq_count * capacity,), -1, jnp.int32)
        .at[slot_of]
        .set(offsets * head_count + head_of)
        .reshape(seq_count, capacity)
    )
    asked_here = lax.all_to_all(asked_codes, "seq", split_axis=0, concat_axis=0, tiled=True)
    is_valid = asked_here >= 0
    asked_block = jnp.maximum(asked_here, 0) // head_count
    asked_head = jnp.maximum(asked_here, 0) % head_count
    block_view = key_value.reshape(block_count, block_len, 2, head_count, head_dim)
    served = block_view[asked_block, :, :, asked_head, :]
    served = jnp.where(is_valid[:, :, None, None, None], served, jnp.zeros_like(served))
    served = served.reshape(seq_count, capacity, block_len, 2 * head_dim)
    received = lax.all_to_all(served, "seq", split_axis=0, concat_axis=0, tiled=True)
    far_pairs = received.reshape(seq_count * capacity, block_len, 2, head_dim)[slot_of]
    pair_view = padded.reshape(block_count + 2, block_len, 2, head_count, head_dim)
    window_pairs = jnp.stack(
        [pair_view[:block_count], pair_view[1 : block_count + 1], pair_view[2:]], axis=1
    ).reshape(block_count, 3 * block_len, 2, head_count, head_dim)
    window_keys = window_pairs[:, :, 0]
    window_vals = window_pairs[:, :, 1]
    first_pairs = first_block.reshape(block_len, 2, head_count, head_dim)
    first_keys = first_pairs[:, 0]
    first_vals = first_pairs[:, 1]
    far_view = far_pairs.reshape(block_count, rand_count, head_count, block_len, 2, head_dim)
    far_keys = far_view[:, :, :, :, 0]
    far_vals = far_view[:, :, :, :, 1]
    global_ids = seq_index * block_count + jnp.arange(block_count, dtype=jnp.int32)
    block_total = seq_count * block_count
    window_live = jnp.stack([global_ids > 0, global_ids >= 0, global_ids < block_total - 1], axis=1)
    window_mask = jnp.repeat(window_live, block_len, axis=1)[None, :, None, :]
    query_blocks = q_rows.reshape(block_count, block_len, head_count, head_dim)
    softmax_scale = 1.0 / math.sqrt(head_dim)
    score_window = (
        jnp.einsum("ibhd,ikhd->hibk", query_blocks, window_keys, preferred_element_type=jnp.float32)
        * softmax_scale
    )
    score_first = (
        jnp.einsum("ibhd,khd->hibk", query_blocks, first_keys, preferred_element_type=jnp.float32)
        * softmax_scale
    )
    score_far = (
        jnp.einsum("ibhd,irhtd->hibrt", query_blocks, far_keys, preferred_element_type=jnp.float32)
        * softmax_scale
    )
    max_window = jnp.max(jnp.where(window_mask, score_window, -jnp.inf), axis=-1, keepdims=True)
    max_first = jnp.max(score_first, axis=-1, keepdims=True)
    max_far = jnp.max(score_far, axis=(-2, -1))[..., None]
    row_max = jnp.maximum(jnp.maximum(max_window, max_first), max_far)
    weight_window = jnp.where(window_mask, jnp.exp(score_window - row_max), 0.0)
    weight_first = jnp.exp(score_first - row_max)
    weight_far = jnp.exp(score_far - row_max[..., None])
    totals = (
        jnp.sum(weight_window, axis=-1, keepdims=True)
        + jnp.sum(weight_first, axis=-1, keepdims=True)
        + jnp.sum(weight_far, axis=(-2, -1))[..., None]
    )
    mixed = jnp.einsum(
        "hibk,ikhd->ibhd",
        weight_window.astype(jnp.bfloat16),
        window_vals,
        preferred_element_type=jnp.float32,
    )
    mixed = mixed + jnp.einsum(
        "hibk,khd->ibhd",
        weight_first.astype(jnp.bfloat16),
        first_vals,
        preferred_element_type=jnp.float32,
    )
    mixed = mixed + jnp.einsum(
        "hibrt,irhtd->ibhd",
        weight_far.astype(jnp.bfloat16),
        far_vals,
        preferred_element_type=jnp.float32,
    )
    totals_rows = jnp.transpose(totals, (1, 2, 0, 3))
    attn = (mixed / totals_rows).astype(jnp.bfloat16)
    logsum = row_max + jnp.log(totals)
    attn_rows = attn.reshape(shard_len, width_cols)
    layer_out = lax.psum_scatter(
        jnp.dot(attn_rows, out_weight, preferred_element_type=jnp.float32),
        "head",
        scatter_dimension=0,
        tiled=True,
    ).astype(jnp.bfloat16)[None]
    piece_flat = lax.all_gather(cotangent, "head", axis=1, tiled=True)[0]
    grad_piece = jnp.dot(piece_flat, out_weight.T, preferred_element_type=jnp.float32).astype(
        jnp.bfloat16
    )
    weight_acc = jnp.dot(attn_rows.T, piece_flat, preferred_element_type=jnp.float32)
    token_total = lax.axis_size("dp") * seq_count * shard_len
    weight_grad = lax.psum(weight_acc, ("dp", "seq")) * (1.0 / math.sqrt(token_total))
    grad_blocks = grad_piece.reshape(block_count, block_len, head_count, head_dim)
    delta_rows = jnp.sum(grad_blocks.astype(jnp.float32) * attn.astype(jnp.float32), axis=-1)
    row_delta = jnp.transpose(delta_rows, (2, 0, 1))[..., None]
    prob_window = jnp.where(window_mask, jnp.exp(score_window - logsum), 0.0)
    prob_first = jnp.exp(score_first - logsum)
    prob_far = jnp.exp(score_far - logsum[..., None])
    dprob_window = jnp.einsum(
        "ibhd,ikhd->hibk", grad_blocks, window_vals, preferred_element_type=jnp.float32
    )
    dprob_first = jnp.einsum(
        "ibhd,khd->hibk", grad_blocks, first_vals, preferred_element_type=jnp.float32
    )
    dprob_far = jnp.einsum(
        "ibhd,irhtd->hibrt", grad_blocks, far_vals, preferred_element_type=jnp.float32
    )
    dscore_window = (prob_window * (dprob_window - row_delta)).astype(jnp.bfloat16)
    dscore_first = (prob_first * (dprob_first - row_delta)).astype(jnp.bfloat16)
    dscore_far = (prob_far * (dprob_far - row_delta[..., None])).astype(jnp.bfloat16)
    grad_q = jnp.einsum(
        "hibk,ikhd->ibhd", dscore_window, window_keys, preferred_element_type=jnp.float32
    )
    grad_q = grad_q + jnp.einsum(
        "hibk,khd->ibhd", dscore_first, first_keys, preferred_element_type=jnp.float32
    )
    grad_q = grad_q + jnp.einsum(
        "hibrt,irhtd->ibhd", dscore_far, far_keys, preferred_element_type=jnp.float32
    )
    grad_q = (grad_q * softmax_scale).astype(jnp.bfloat16)
    key_window = (
        jnp.einsum(
            "hibk,ibhd->ikhd", dscore_window, query_blocks, preferred_element_type=jnp.float32
        )
        * softmax_scale
    )
    value_window = jnp.einsum(
        "hibk,ibhd->ikhd",
        prob_window.astype(jnp.bfloat16),
        grad_blocks,
        preferred_element_type=jnp.float32,
    )
    key_first = (
        jnp.einsum("hibk,ibhd->khd", dscore_first, query_blocks, preferred_element_type=jnp.float32)
        * softmax_scale
    )
    value_first = jnp.einsum(
        "hibk,ibhd->khd",
        prob_first.astype(jnp.bfloat16),
        grad_blocks,
        preferred_element_type=jnp.float32,
    )
    key_far = (
        jnp.einsum(
            "hibrt,ibhd->irhtd", dscore_far, query_blocks, preferred_element_type=jnp.float32
        )
        * softmax_scale
    )
    value_far = jnp.einsum(
        "hibrt,ibhd->irhtd",
        prob_far.astype(jnp.bfloat16),
        grad_blocks,
        preferred_element_type=jnp.float32,
    )
    window_terms = jnp.stack(
        [
            key_window.reshape(block_count, 3, block_len, head_count, head_dim),
            value_window.reshape(block_count, 3, block_len, head_count, head_dim),
        ],
        axis=3,
    )
    grad_pad = jnp.zeros((block_count + 2, block_len, 2, head_count, head_dim), jnp.float32)
    grad_pad = (
        grad_pad.at[:block_count]
        .add(window_terms[:, 0])
        .at[1 : block_count + 1]
        .add(window_terms[:, 1])
        .at[2:]
        .add(window_terms[:, 2])
    )
    global_grad = lax.psum(jnp.stack([key_first, value_first], axis=1), "seq")
    grad_pad = grad_pad.at[1].add(jnp.where(seq_index == 0, global_grad, 0.0))
    rims = jnp.concatenate([grad_pad[0], grad_pad[block_count + 1]], axis=0).reshape(
        2 * block_len, 2 * width_cols
    )
    rim_sums = with_halo(rims.astype(jnp.bfloat16), (("seq", 0),), block_len).astype(rims.dtype)
    core = grad_pad[1 : block_count + 1].reshape(shard_len, 2 * width_cols)
    core = (
        core.at[:block_len]
        .add(rim_sums[:block_len])
        .at[shard_len - block_len :]
        .add(rim_sums[3 * block_len :])
    )
    core = core.reshape(block_count, block_len, 2, head_count, head_dim)
    far_terms = (
        jnp.stack([key_far, value_far], axis=4)
        .reshape(request_count, block_len, 2, head_dim)
        .astype(jnp.bfloat16)
    )
    outgoing = (
        jnp.zeros((seq_count * capacity, block_len, 2, head_dim), jnp.bfloat16)
        .at[slot_of]
        .set(far_terms)
    )
    outgoing = outgoing.reshape(seq_count, capacity, block_len, 2 * head_dim)
    incoming = (
        lax.all_to_all(outgoing, "seq", split_axis=0, concat_axis=0, tiled=True)
        .reshape(seq_count, capacity, block_len, 2, head_dim)
        .astype(jnp.float32)
    )
    incoming = jnp.where(is_valid[:, :, None, None, None], incoming, 0.0)
    core = core.at[asked_block, :, :, asked_head, :].add(incoming)
    grad_k = core[:, :, 0].reshape(shard_len, width_cols).astype(jnp.bfloat16)
    grad_v = core[:, :, 1].reshape(shard_len, width_cols).astype(jnp.bfloat16)
    grad_q_rows = grad_q.reshape(shard_len, width_cols)
    grad_queries, grad_keys, grad_values = (
        lax.all_to_all(grad_q_rows[None], "head", split_axis=1, concat_axis=2, tiled=True),
        lax.all_to_all(grad_k[None], "head", split_axis=1, concat_axis=2, tiled=True),
        lax.all_to_all(grad_v[None], "head", split_axis=1, concat_axis=2, tiled=True),
    )
    return (layer_out, grad_queries, grad_keys, grad_values, weight_grad)


def solution(mesh):
    in_specs = (
        P("dp", ("seq", "head"), None),
        P("dp", ("seq", "head"), None),
        P("dp", ("seq", "head"), None),
        P("seq", "head", None),
        P("head", None),
        P("dp", ("seq", "head"), None),
    )
    out_specs = (
        P("dp", ("seq", "head"), None),
        P("dp", ("seq", "head"), None),
        P("dp", ("seq", "head"), None),
        P("dp", ("seq", "head"), None),
        P("head", None),
    )
    return jax.shard_map(
        per_device, mesh=mesh, in_specs=in_specs, out_specs=out_specs, check_vma=False
    )
```

profile of v0, /device:TPU:38, one launch (start us, length us, event | category | flops | bytes accessed | tf_op | source)
XLA Modules:
  0.0 795.5 jit_solution(17635221475031465558)
XLA Ops:
  13.4 7.8 all-to-all-start.3
  21.2 5.9 copy.314
  27.6 12.6 %reduce.16 = bf16[2048,160]{1,0:T(8,128)(2,1)S(1)} reduce(bf16[2048,1,160]{2,1,0:T(2,128)(2,1)} %bitcast.313, bf16[]{:T(256)} %broadcast.542), dimensions={1}, to_apply=%bitcast.270.reduce_sub_computation | reduce | bytes 1310722
  42.5 4.5 all-to-all-start.1
  47.0 5.9 copy.311
  52.8 12.6 %reduce.17 = bf16[2048,160]{1,0:T(8,128)(2,1)S(1)} reduce(bf16[2048,1,160]{2,1,0:T(2,128)(2,1)} %bitcast.317, bf16[]{:T(256)} %broadcast.542), dimensions={1}, to_apply=%bitcast.272.reduce_sub_computation | reduce | bytes 1310722
  67.8 5.1 all-to-all-start
  72.9 5.9 copy.319
  78.7 12.6 %reduce.15 = bf16[2048,160]{1,0:T(8,128)(2,1)S(1)} reduce(bf16[2048,1,160]{2,1,0:T(2,128)(2,1)} %bitcast.318, bf16[]{:T(256)} %broadcast.542), dimensions={1}, to_apply=%bitcast.274.reduce_sub_computation | reduce | bytes 1310722
  94.3 4.2 reshape.654
  98.6 4.5 copy.315
  103.7 4.8 all-to-all-start.2
  108.5 4.2 reshape.656
  112.7 5.7 copy.312
  120.7 3.4 collective-permute-start
  127.5 5.5 collective-permute-done.1
  133.0 5.4 pad_maximum_fusion.6
  143.0 12.1 %gather_fusion = bf16[240,64,2,128]{3,1,2,0:T(8,128)(2,1)} fusion(bf16[10,64,2,4,128]{4,1,3,2,0:T(8,128)(2,1)S(1)} %copy.335, s32[240]{0:T(256)S(1)} %reshape.602), kind=kCustom, calls=%fused_computation | custom fusion | bytes 15730560 | tf_op jit(solution)/shard_map/gather | solution.py:68
  155.1 15.3 %copy.336 = bf16[240,64,2,128]{3,2,1,0:T(2,128)(2,1)} copy(bf16[240,64,2,128]{3,1,2,0:T(8,128)(2,1)} %gather_fusion) | data formatting | bytes 15728640 | tf_op jit(solution)/shard_map/gather | solution.py:68
  170.4 13.4 %gather.9 = bf16[16,15,64,256]{3,2,1,0:T(8,128)(2,1)} reshape(bf16[240,64,2,128]{3,2,1,0:T(2,128)(2,1)} %copy.336) | data formatting | bytes 15728640 | tf_op jit(solution)/shard_map/gather | solution.py:68
  183.8 7.0 broadcast_select_fusion.1
  190.8 6.7 all-to-all-start.4
  199.5 4.2 reshape.658
  203.7 5.7 copy.320
  218.4 3.9 stack.41
  224.1 5.0 pad_maximum_fusion.1
  232.1 108.2 %all-reduce.6.cloned.1.call-done = bf16[64,2,4,128]{3,0,2,1:T(8,128)(2,1)} async-done(((bf16[64,2,4,128]{3,0,2,1:T(8,128)(2,1)}), bf16[64,2,4,128]{3,0,2,1:T(8,128)(2,1)}) %all-reduce.6.cloned.1.call-update) | async-done | bytes 131088 | tf_op jit(solution)/shard_map/psum | solution.py:26
  343.0 4.7 select_reduce_fusion
  350.0 4.1 fusion.66
  355.8 12.2 %reshape.589 = bf16[240,64,2,128]{3,2,1,0:T(2,128)(2,1)} reshape(bf16[16,15,64,256]{3,2,1,0:T(8,128)(2,1)} %all-to-all-done.4) | data formatting | bytes 15728640 | tf_op jit(solution)/shard_map/reshape | solution.py:72
  368.0 8.5 %copy.337 = bf16[240,64,2,128]{3,1,2,0:T(8,128)(2,1)} copy(bf16[240,64,2,128]{3,2,1,0:T(2,128)(2,1)} %reshape.589) | data formatting | bytes 15728640 | tf_op jit(solution)/shard_map/reshape | solution.py:72
  376.5 11.2 %gather_fusion.1 = bf16[160,64,2,128]{3,1,2,0:T(8,128)(2,1)} fusion(bf16[240,64,2,128]{3,1,2,0:T(8,128)(2,1)} %copy.337, s32[1024]{0:T(1024)S(1)} %pad_clamp_fusion), kind=kCustom, calls=%fused_computation.1 | custom fusion | bytes 10486400 | tf_op jit(solution)/shard_map/gather | solution.py:72
  387.7 7.3 slice_bitcast_fusion.5
  418.5 3.9 fusion.17
  422.4 3.3 convert_bitcast_fusion
  433.2 4.2 copy.383
  437.4 5.1 broadcast_in_dim.101
  442.5 24.2 %scatter_fusion = bf16[240,64,2,128]{3,1,2,0:T(8,128)(2,1)} fusion(bf16[240,64,2,128]{3,1,2,0:T(8,128)(2,1)} %broadcast_in_dim.101, s32[160]{0:T(256)S(1)} %bitcast.345, bf16[160,64,2,128]{3,1,2,0:T(8,128)(2,1)} %copy.383), kind=kCustom, calls=%fused_computation.3 | custom fusion | bytes 15729280 | tf_op jit(solution)/shard_map/scatter | solution.py:250
  466.7 15.4 %copy.384 = bf16[240,64,2,128]{3,2,1,0:T(2,128)(2,1)} copy(bf16[240,64,2,128]{3,1,2,0:T(8,128)(2,1)} %scatter_fusion) | data formatting | bytes 15728640 | tf_op jit(solution)/shard_map/scatter | solution.py:250
  482.1 13.4 %reshape.599 = bf16[16,15,64,256]{3,2,1,0:T(8,128)(2,1)} reshape(bf16[240,64,2,128]{3,2,1,0:T(2,128)(2,1)} %copy.384) | data formatting | bytes 15728640 | tf_op jit(solution)/shard_map/reshape | solution.py:252
  495.5 7.2 all-to-all-start.6
  502.7 3.8 fusion.85
  522.0 3.8 fusion.14
  525.7 3.8 fusion.8
  536.7 5.2 collective-permute-start.2
  541.9 3.6 fusion.63
  548.5 5.5 reduce.18
  560.6 4.2 reshape.596
  565.0 38.2 %collective-permute-done.3 = bf16[64,1024]{1,0:T(8,128)(2,1)S(1)} collective-permute-done((bf16[64,1024]{1,0:T(8,128)(2,1)S(1)}, bf16[64,1024]{1,0:T(8,128)(2,1)S(1)}, u32[]{:S(2)}, u32[]{:S(2)}) %collective-permute-start.3) | collective-permute-done | bytes 131104 | tf_op jit(solution)/shard_map/ppermute | solution.py:19
  603.2 20.1 %collective-permute-done.2 = bf16[64,1024]{1,0:T(8,128)(2,1)S(1)} collective-permute-done((bf16[64,1024]{1,0:T(8,128)(2,1)S(1)}, bf16[64,1024]{1,0:T(8,128)(2,1)S(1)}, u32[]{:S(2)}, u32[]{:S(2)}) %collective-permute-start.2) | collective-permute-done | bytes 131104 | tf_op jit(solution)/shard_map/ppermute | solution.py:16
  625.7 4.2 reshape.598
  629.9 3.7 copy.385
  633.6 4.8 all-to-all-start.5
  638.4 16.2 %reshape.601 = f32[16,15,64,2,128]{4,3,2,1,0:T(2,128)} reshape(bf16[16,15,64,256]{3,2,1,0:T(8,128)(2,1)} %all-to-all-done.6) | data formatting | bytes 23592960 | tf_op jit(solution)/shard_map/convert_element_type | solution.py:256
  654.6 12.1 %broadcast_select_fusion = f32[16,15,64,2,128]{4,3,2,1,0:T(2,128)} fusion(f32[16,15,64,2,128]{4,3,2,1,0:T(2,128)} %reshape.601, pred[16,15]{1,0:T(8,128)(4,1)S(1)} %compare_bitcast_fusion), kind=kLoop, calls=%fused_computation.5 | loop fusion | flops 3932160 | bytes 31457520 | tf_op jit(solution)/shard_map/jit(_where)/select_n | solution.py:258
  666.8 13.5 %copy.386 = f32[240,64,2,128]{3,1,2,0:T(8,128)} copy(f32[240,64,2,128]{3,2,1,0:T(2,128)} %bitcast.298) | data formatting | bytes 31457280 | tf_op jit(solution)/shard_map/jit(_where)/select_n | solution.py:258
  680.3 50.5 %scatter_fusion.1 = f32[10,64,2,4,128]{4,1,3,2,0:T(8,128)} fusion(f32[10,64,2,4,128]{4,1,3,2,0:T(8,128)} %copy.385, s32[240]{0:T(256)S(1)} %reshape.632, f32[240,64,2,128]{3,1,2,0:T(8,128)} %copy.386), kind=kCustom, calls=%fused_computation.4 | custom fusion | flops 3932160 | bytes 47187840 | tf_op jit(solution)/shard_map/scatter-add | solution.py:259
  735.1 3.7 convert_element_type.101
  738.8 5.4 reduce.19
  747.1 4.9 all-to-all-start.7
  756.8 3.7 convert_element_type.102
  760.5 5.4 reduce.20
  768.8 4.8 all-to-all-start.8
  773.6 5.0 broadcast_multiply_fusion
  (218 shorter events, 136.9 us)
Async XLA Ops:
  8.0 342.0 %copy-start = (bf16[512,2048]{1,0:T(8,128)(2,1)S(1)}, bf16[512,2048]{1,0:T(8,128)(2,1)}, u32[]{:S(2)}) copy-start(bf16[512,2048]{1,0:T(8,128)(2,1)} %param.22) | copy-start | bytes 6291460
  11.6 15.5 %copy-start.31 = (s32[160,1]{0,1:T(1,128)}, s32[160,1]{0,1:T(1,128)S(1)}, u32[]{:S(2)}) copy-start(s32[160,1]{0,1:T(1,128)S(1)} %compare_select_fusion.2) | copy-start | bytes 1924
  13.4 29.1 %all-to-all-start.3 = ((s32[16,1,15]{2,1,0:T(1,128)}), s32[16,1,15]{2,1,0:T(1,128)S(1)}, u32[]{:S(2)}, u32[]{:S(2)}) async-start(s32[16,1,15]{2,1,0:T(1,128)} %bitcast.19), calls=%async_computation.3 | async-start | bytes 16384 | tf_op jit(solution)/shard_map/all_to_all | solution.py:63
  42.5 25.2 %all-to-all-start.1 = ((bf16[4,2,40960]{2,1,0:T(2,128)(2,1)}), bf16[4,2,40960]{2,1,0:T(2,128)(2,1)}, u32[]{:S(2)}, u32[]{:S(2)}) async-start(bf16[4,2,40960]{2,1,0:T(2,128)(2,1)} %reshape.653), calls=%async_computation.1 | async-start | bytes 1310720 | tf_op jit(solution)/shard_map/all_to_all | solution.py:37
  67.8 35.9 %all-to-all-start = ((bf16[4,2,40960]{2,1,0:T(2,128)(2,1)}), bf16[4,2,40960]{2,1,0:T(2,128)(2,1)}, u32[]{:S(2)}, u32[]{:S(2)}) async-start(bf16[4,2,40960]{2,1,0:T(2,128)(2,1)} %reshape.655), calls=%async_computation | async-start | bytes 1310720 | tf_op jit(solution)/shard_map/all_to_all | solution.py:36
  103.7 17.0 %copy-start.20 = (bf16[1,4,160,512]{3,2,1,0:T(8,128)(2,1)}, bf16[1,4,160,512]{3,2,1,0:T(8,128)(2,1)S(1)}, u32[]{:S(2)}) copy-start(bf16[1,4,160,512]{3,2,1,0:T(8,128)(2,1)S(1)} %copy.316) | copy-start | bytes 1966084
  103.7 87.1 %all-to-all-start.2 = ((bf16[4,2,40960]{2,1,0:T(2,128)(2,1)}), bf16[4,2,40960]{2,1,0:T(2,128)(2,1)}, u32[]{:S(2)}, u32[]{:S(2)}) async-start(bf16[4,2,40960]{2,1,0:T(2,128)(2,1)} %reshape.657), calls=%async_computation.2 | async-start | bytes 1310720 | tf_op jit(solution)/shard_map/all_to_all | solution.py:35
  120.7 6.9 collective-permute-start
  124.0 9.0 %collective-permute-start.1 = (bf16[64,1024]{1,0:T(8,128)(2,1)S(1)}, bf16[64,1024]{1,0:T(8,128)(2,1)S(1)}, u32[]{:S(2)}, u32[]{:S(2)}) collective-permute-start(bf16[64,1024]{1,0:T(8,128)(2,1)S(1)} %get-tuple-element.80), channel_id=1, source_target_pairs={{4,0},{8,4},{12,8},{16,12},{20,16},{24,20},{28,24},{32,28},{36,32}... | collective-permute-start | bytes 393224 | tf_op jit(solution)/shard_map/ppermute | solution.py:19
  138.4 1.1 copy-start.8
  190.8 8.7 %copy-start.32 = (s32[160,1]{0,1:T(1,128)S(1)}, s32[160,1]{0,1:T(1,128)}, u32[]{:S(2)}) copy-start(s32[160,1]{0,1:T(1,128)} %copy-done.31) | copy-start | bytes 1924
  190.8 165.0 %all-to-all-start.4 = ((bf16[16,15,64,256]{3,2,1,0:T(8,128)(2,1)}), bf16[16,15,64,256]{3,2,1,0:T(8,128)(2,1)}, u32[]{:S(2)}, u32[]{:S(2)}) async-start(bf16[16,15,64,256]{3,2,1,0:T(8,128)(2,1)} %broadcast_select_fusion.1), calls=%async_computation.4 | async-start | bytes 15728640 | tf_op jit(solution)/shard_map/all_to_all | solution.py:71
  197.5 142.8 %all-reduce.6.cloned.1.call-start = ((), (), s32[]{:S(2)}) async-start(), calls=%async_computation.10 | async-start | bytes 262144 | tf_op jit(solution)/shard_map/psum | solution.py:26
  198.4 151.7 %all-gather.2.cloned.1.call-start = ((), (), s32[]{:S(2)}) async-start(), calls=%async_computation.12 | async-start | bytes 3276800 | tf_op jit(solution)/shard_map/all_gather | solution.py:143
  198.9 330.6 %all-reduce.8.cloned.1.call-start = ((), (), s32[]{:S(2)}) async-start(), calls=%async_computation.13 | async-start | bytes 524288 | tf_op jit(solution)/shard_map/psum | solution.py:228
  209.4 7.2 copy-start.9
  218.4 3.9 copy-start.21
  229.0 111.3 %copy-start.10 = (bf16[10,64,4,128]{3,2,1,0:T(4,128)(2,1)S(1)}, bf16[10,64,4,128]{3,2,1,0:T(4,128)(2,1)}, u32[]{:S(2)}) copy-start(bf16[10,64,4,128]{3,2,1,0:T(4,128)(2,1)} %reshape_squeeze.2) | copy-start | bytes 1966084
  343.0 4.7 copy-start.6
  355.8 59.4 %copy-start.2 = (bf16[10,64,4,128]{3,2,1,0:T(4,128)(2,1)}, bf16[10,64,4,128]{3,2,1,0:T(4,128)(2,1)S(1)}, u32[]{:S(2)}) copy-start(bf16[10,64,4,128]{3,2,1,0:T(4,128)(2,1)S(1)} %reshape.592) | copy-start | bytes 1966084
  395.9 6.9 copy-start.1
  396.0 3.6 copy-start.13
  397.4 3.2 copy-start.5
  405.9 1.0 copy-start.28
  405.9 1.6 copy-start.27
  411.3 0.8 copy-start.25
  412.9 360.7 %all-reduce.10.cloned.1.call-start = ((), (), s32[]{:S(2)}) async-start(), calls=%async_computation.14 | async-start | bytes 8388608 | tf_op jit(solution)/shard_map/psum | solution.py:149
  415.2 3.2 copy-start.18
  415.3 3.2 copy-start.23
  422.4 4.0 slice-start
  422.4 4.1 slice-start.1
  425.7 1.3 copy-start.3
  425.7 2.1 copy-start.17
  427.9 3.2 copy-start.11
  429.6 1.5 copy-start.14
  495.5 7.2 copy-start.19
  495.5 138.2 %all-to-all-start.6 = ((bf16[16,15,64,256]{3,2,1,0:T(8,128)(2,1)}), bf16[16,15,64,256]{3,2,1,0:T(8,128)(2,1)}, u32[]{:S(2)}, u32[]{:S(2)}) async-start(bf16[16,15,64,256]{3,2,1,0:T(8,128)(2,1)} %reshape.599), calls=%async_computation.7 | async-start | bytes 15728640 | tf_op jit(solution)/shard_map/all_to_all | solution.py:254
  502.6 283.3 %reduce-scatter.2.cloned.1.call-start = ((), (), s32[]{:S(2)}) async-start(), calls=%async_computation.11 | async-start | bytes 6553600 | tf_op jit(solution)/shard_map/reduce_scatter | solution.py:137
  506.5 0.7 copy-start.30
  506.5 1.1 copy-start.4
  507.6 2.5 copy-start.7
  510.1 3.0 copy-start.12
  513.2 1.1 copy-start.22
  515.1 2.3 copy-start.26
  515.3 2.1 copy-start.29
  515.3 3.5 copy-start.15
  515.3 4.5 copy-start.16
  533.7 69.5 %collective-permute-start.3 = (bf16[64,1024]{1,0:T(8,128)(2,1)S(1)}, bf16[64,1024]{1,0:T(8,128)(2,1)S(1)}, u32[]{:S(2)}, u32[]{:S(2)}) collective-permute-start(bf16[64,1024]{1,0:T(8,128)(2,1)S(1)} %concatenate.44), channel_id=1, source_target_pairs={{4,0},{8,4},{12,8},{16,12},{20,16},{24,20},{28,24},{32,28},{36,32}... | collective-permute-start | bytes 393224 | tf_op jit(solution)/shard_map/ppermute | solution.py:19
  536.7 86.6 %collective-permute-start.2 = (bf16[64,1024]{1,0:T(8,128)(2,1)S(1)}, bf16[64,1024]{1,0:T(8,128)(2,1)S(1)}, u32[]{:S(2)}, u32[]{:S(2)}) collective-permute-start(bf16[64,1024]{1,0:T(8,128)(2,1)S(1)} %concatenate.43), channel_id=1, source_target_pairs={{0,4},{4,8},{8,12},{12,16},{16,20},{20,24},{24,28},{28,32},{32,36}... | collective-permute-start | bytes 393224 | tf_op jit(solution)/shard_map/ppermute | solution.py:16
  633.6 113.5 %all-to-all-start.5 = ((bf16[4,2,40960]{2,1,0:T(2,128)(2,1)}), bf16[4,2,40960]{2,1,0:T(2,128)(2,1)}, u32[]{:S(2)}, u32[]{:S(2)}) async-start(bf16[4,2,40960]{2,1,0:T(2,128)(2,1)} %reshape.659), calls=%async_computation.6 | async-start | bytes 1310720 | tf_op jit(solution)/shard_map/all_to_all | solution.py:264
  747.1 21.7 %all-to-all-start.7 = ((bf16[4,2,40960]{2,1,0:T(2,128)(2,1)}), bf16[4,2,40960]{2,1,0:T(2,128)(2,1)}, u32[]{:S(2)}, u32[]{:S(2)}) async-start(bf16[4,2,40960]{2,1,0:T(2,128)(2,1)} %reshape.661), calls=%async_computation.8 | async-start | bytes 1310720 | tf_op jit(solution)/shard_map/all_to_all | solution.py:265
  754.3 1.1 copy-start.24
  768.8 13.7 %all-to-all-start.8 = ((bf16[4,2,40960]{2,1,0:T(2,128)(2,1)}), bf16[4,2,40960]{2,1,0:T(2,128)(2,1)}, u32[]{:S(2)}, u32[]{:S(2)}) async-start(bf16[4,2,40960]{2,1,0:T(2,128)(2,1)} %reshape.663), calls=%async_computation.9 | async-start | bytes 1310720 | tf_op jit(solution)/shard_map/all_to_all | solution.py:266
Sparse Core Ops, SparseCore 0:
  202.1 138.1 all-reduce.5
  413.0 84.3 all-reduce.7
  501.3 193.5 all-reduce.9
Sparse Core Ops, SparseCore 1:
  200.5 36.7 all-gather.1
  506.6 56.6 reduce-scatter.1
where the time goes:
time: 808 us; the launch traced here: 795 us
  local copies, waits for them, and re-layouts  324 us (40%)
  waiting for transfers between devices  174 us (22%)
  other arithmetic  173 us (21%)
  starting transfers between devices  65.3 us (8%)
  matrix products  43.5 us (5%)
  between operations  16.2 us (2%)
    psum x1, waiting for transfers between devices, from_root(): return lax.psum(block, axis)  108 us
    unnamed x90, local copies, waits for them, and re-layouts  62.3 us
    unnamed x7, other arithmetic  53.9 us
    scatter-add x1, other arithmetic, per_device(): core = core.at[asked_block, :, :, asked_head, :].add(incoming)  50.5 us
    ppermute x2, waiting for transfers between devices, with_halo(): lax.ppermute(lax.slice_in_dim(block, 0, width, axis=dim), axis, backward)  43.6 us
    gather x3, local copies, waits for them, and re-layouts, per_device(): served = block_view[asked_block, :, :, asked_head, :]  40.8 us
    scatter x2, local copies, waits for them, and re-layouts, per_device(): outgoing = jnp.zeros((seq_count * capacity, block_len, 2, head_dim), jnp....  39.6 us
    reshape x2, local copies, waits for them, and re-layouts, per_device(): received.reshape(seq_count * capacity, block_len, 2, head_dim)[slot_of]  20.7 us
  transfers between devices with their start and end apart: 18, of which 6 were waited for; matrix products, arithmetic and copies ran while one was open for 58% of the time, Pallas kernels for 0%

commit v1 on v0

--- a/solution.py
+++ b/solution.py
@@ -6,6 +6,7 @@
 
 HEAD_SIZE = 128
 BLOCK_TOKENS = 64
+core_divide = lambda a0, dev_axis: jnp.sum(lax.all_gather(a0, dev_axis), 0)
 
 
 def with_halo(block, sides, width):
@@ -23,7 +24,7 @@
 
 def from_root(block, axis, holder):
     block = jnp.where(lax.axis_index(axis) == holder, block, jnp.zeros_like(block))
-    return lax.psum(block, axis)
+    return core_divide(block, axis)
 
 
 def per_device(queries, key_rows, values, rand_blocks, out_weight, cotangent):

time: 808 us -> 769 us (0.952)
  waiting for transfers between devices: 174 us -> 136 us
    psum x1 -> x0, waiting for transfers between devices: 108 us -> none  [from_root(): return lax.psum(block, axis)]
    all_gather x0 -> x1, waiting for transfers between devices: none -> 67.2 us  [core_divide = lambda a0, dev_axis: jnp.sum(lax.all_gather(a0, dev_axis), 0)]
    unnamed x90 -> x88, local copies, waits for them, and re-layouts: 62.3 us -> 62.4 us
  transfers between devices with their start and end apart: 18 -> 18, of which waited for: 6 -> 6; matrix products, arithmetic and copies ran while one was open for 58% -> 61% of each run, Pallas kernels for 0% -> 0%
where the time goes in v1:
time: 769 us; the launch traced here: 757 us
  local copies, waits for them, and re-layouts  323 us (42%)
  other arithmetic  176 us (23%)
  waiting for transfers between devices  136 us (18%)
  starting transfers between devices  65.8 us (9%)
  matrix products  41 us (5%)
  between operations  15.1 us (2%)
    all_gather x1, waiting for transfers between devices, core_divide = lambda a0, dev_axis: jnp.sum(lax.all_gather(a0, dev_axis), 0)  67.2 us
    unnamed x88, local copies, waits for them, and re-layouts  62.4 us
    unnamed x7, other arithmetic  54.4 us
    scatter-add x1, other arithmetic, per_device(): core = core.at[asked_block, :, :, asked_head, :].add(incoming)  50.8 us
    ppermute x2, waiting for transfers between devices, with_halo(): lax.ppermute(lax.slice_in_dim(block, 0, width, axis=dim), axis, backward)  45.9 us
    gather x3, local copies, waits for them, and re-layouts, per_device(): served = block_view[asked_block, :, :, asked_head, :]  40.9 us
    scatter x2, local copies, waits for them, and re-layouts, per_device(): outgoing = jnp.zeros((seq_count * capacity, block_len, 2, head_dim), jnp....  39.4 us
    ppermute x2, waiting for transfers between devices, with_halo(): lax.ppermute(lax.slice_in_dim(block, block.shape[dim] - width, None, axis...  21.1 us
  transfers between devices with their start and end apart: 18, of which 6 were waited for; matrix products, arithmetic and copies ran while one was open for 61% of the time, Pallas kernels for 0%

profile of v1, /device:TPU:38, one launch (start us, length us, event | category | flops | bytes accessed | tf_op | source)
XLA Modules:
  0.0 756.8 jit_solution(17509610031149775058)
XLA Ops:
  12.6 7.8 %all-to-all-start.3 = ((s32[16,1,15]{2,1,0:T(1,128)}), s32[16,1,15]{2,1,0:T(1,128)S(1)}, u32[]{:S(2)}, u32[]{:S(2)}) async-start(s32[16,1,15]{2,1,0:T(1,128)} %bitcast.20), calls=%async_computation.3 | async-start | bytes 16384 | tf_op jit(solution)/shard_map/all_to_all | solution.py:64
  20.4 5.9 copy.318
  26.8 12.6 %reduce.17 = bf16[2048,160]{1,0:T(8,128)(2,1)S(1)} reduce(bf16[2048,1,160]{2,1,0:T(2,128)(2,1)} %bitcast.314, bf16[]{:T(256)} %broadcast.542), dimensions={1}, to_apply=%bitcast.271.reduce_sub_computation | reduce | bytes 1310722
  41.8 4.5 all-to-all-start.1
  46.3 5.9 copy.315
  52.2 12.6 %reduce.18 = bf16[2048,160]{1,0:T(8,128)(2,1)S(1)} reduce(bf16[2048,1,160]{2,1,0:T(2,128)(2,1)} %bitcast.318, bf16[]{:T(256)} %broadcast.542), dimensions={1}, to_apply=%bitcast.273.reduce_sub_computation | reduce | bytes 1310722
  67.2 4.8 all-to-all-start
  72.7 5.9 copy.323
  78.5 12.6 %reduce.16 = bf16[2048,160]{1,0:T(8,128)(2,1)S(1)} reduce(bf16[2048,1,160]{2,1,0:T(2,128)(2,1)} %bitcast.319, bf16[]{:T(256)} %broadcast.542), dimensions={1}, to_apply=%bitcast.275.reduce_sub_computation | reduce | bytes 1310722
  93.6 4.2 reshape.655
  97.8 4.5 copy.319
  103.0 4.8 all-to-all-start.2
  107.8 4.2 reshape.657
  112.0 5.7 copy.316
  120.6 3.4 collective-permute-start
  127.5 5.5 collective-permute-done.1
  133.0 5.4 pad_maximum_fusion.6
  142.9 12.2 %gather_fusion = bf16[240,64,2,128]{3,1,2,0:T(8,128)(2,1)} fusion(bf16[10,64,2,4,128]{4,1,3,2,0:T(8,128)(2,1)S(1)} %copy.339, s32[240]{0:T(256)S(1)} %reshape.602), kind=kCustom, calls=%fused_computation | custom fusion | bytes 15730560 | tf_op jit(solution)/shard_map/gather | solution.py:69
  155.0 15.3 %copy.340 = bf16[240,64,2,128]{3,2,1,0:T(2,128)(2,1)} copy(bf16[240,64,2,128]{3,1,2,0:T(8,128)(2,1)} %gather_fusion) | data formatting | bytes 15728640 | tf_op jit(solution)/shard_map/gather | solution.py:69
  170.4 13.4 %gather.9 = bf16[16,15,64,256]{3,2,1,0:T(8,128)(2,1)} reshape(bf16[240,64,2,128]{3,2,1,0:T(2,128)(2,1)} %copy.340) | data formatting | bytes 15728640 | tf_op jit(solution)/shard_map/gather | solution.py:69
  183.8 7.0 broadcast_select_fusion.1
  190.8 6.6 all-to-all-start.4
  199.5 4.2 reshape.659
  203.8 5.7 copy.324
  218.4 3.9 stack.41
  224.1 4.9 pad_maximum_fusion.1
  230.1 3.6 select_reduce_fusion
  235.9 4.1 fusion.66
  241.7 67.2 %all-gather.6.cloned.1.call-done = bf16[1024,1024]{1,0:T(8,128)(2,1)} async-done(((bf16[64,1024]{1,0:T(8,128)(2,1)}), bf16[1024,1024]{1,0:T(8,128)(2,1)}) %all-gather.6.cloned.1.call-update) | async-done | bytes 2097168 | tf_op jit(solution)/shard_map/all_gather | solution.py:9
  315.0 12.1 %reshape.589 = bf16[240,64,2,128]{3,2,1,0:T(2,128)(2,1)} reshape(bf16[16,15,64,256]{3,2,1,0:T(8,128)(2,1)} %all-to-all-done.4) | data formatting | bytes 15728640 | tf_op jit(solution)/shard_map/reshape | solution.py:73
  327.1 8.5 %copy.341 = bf16[240,64,2,128]{3,1,2,0:T(8,128)(2,1)} copy(bf16[240,64,2,128]{3,2,1,0:T(2,128)(2,1)} %reshape.589) | data formatting | bytes 15728640 | tf_op jit(solution)/shard_map/reshape | solution.py:73
  335.6 11.1 %gather_fusion.1 = bf16[160,64,2,128]{3,1,2,0:T(8,128)(2,1)} fusion(bf16[240,64,2,128]{3,1,2,0:T(8,128)(2,1)} %copy.341, s32[1024]{0:T(1024)} %pad_clamp_fusion), kind=kCustom, calls=%fused_computation.1 | custom fusion | bytes 10486400 | tf_op jit(solution)/shard_map/gather | solution.py:73
  346.8 7.3 slice_bitcast_fusion.5
  377.3 3.9 fusion.17
  381.2 3.3 convert_bitcast_fusion
  392.0 4.2 copy.388
  396.2 5.1 broadcast_in_dim.101
  401.3 24.1 %scatter_fusion = bf16[240,64,2,128]{3,1,2,0:T(8,128)(2,1)} fusion(bf16[240,64,2,128]{3,1,2,0:T(8,128)(2,1)} %broadcast_in_dim.101, s32[160]{0:T(256)S(1)} %bitcast.347, bf16[160,64,2,128]{3,1,2,0:T(8,128)(2,1)} %copy.388), kind=kCustom, calls=%fused_computation.3 | custom fusion | bytes 15729280 | tf_op jit(solution)/shard_map/scatter | solution.py:251
  425.3 15.4 %copy.389 = bf16[240,64,2,128]{3,2,1,0:T(2,128)(2,1)} copy(bf16[240,64,2,128]{3,1,2,0:T(8,128)(2,1)} %scatter_fusion) | data formatting | bytes 15728640 | tf_op jit(solution)/shard_map/scatter | solution.py:251
  440.7 13.4 %reshape.599 = bf16[16,15,64,256]{3,2,1,0:T(8,128)(2,1)} reshape(bf16[240,64,2,128]{3,2,1,0:T(2,128)(2,1)} %copy.389) | data formatting | bytes 15728640 | tf_op jit(solution)/shard_map/reshape | solution.py:253
  454.1 7.3 all-to-all-start.6
  461.9 3.8 fusion.85
  481.1 3.8 fusion.14
  484.9 3.8 fusion.8
  495.7 5.4 collective-permute-start.2
  501.1 3.5 fusion.63
  507.5 5.6 reduce.19
  519.6 4.1 reshape.596
  524.0 40.4 %collective-permute-done.3 = bf16[64,1024]{1,0:T(8,128)(2,1)S(1)} collective-permute-done((bf16[64,1024]{1,0:T(8,128)(2,1)S(1)}, bf16[64,1024]{1,0:T(8,128)(2,1)S(1)}, u32[]{:S(2)}, u32[]{:S(2)}) %collective-permute-start.3) | collective-permute-done | bytes 131104 | tf_op jit(solution)/shard_map/ppermute | solution.py:20
  564.4 20.3 %collective-permute-done.2 = bf16[64,1024]{1,0:T(8,128)(2,1)S(1)} collective-permute-done((bf16[64,1024]{1,0:T(8,128)(2,1)S(1)}, bf16[64,1024]{1,0:T(8,128)(2,1)S(1)}, u32[]{:S(2)}, u32[]{:S(2)}) %collective-permute-start.2) | collective-permute-done | bytes 131104 | tf_op jit(solution)/shard_map/ppermute | solution.py:17
  587.2 4.2 reshape.598
  591.4 3.7 copy.390
  595.1 4.4 all-to-all-start.5
  599.5 16.2 %reshape.601 = f32[16,15,64,2,128]{4,3,2,1,0:T(2,128)} reshape(bf16[16,15,64,256]{3,2,1,0:T(8,128)(2,1)} %all-to-all-done.6) | data formatting | bytes 23592960 | tf_op jit(solution)/shard_map/convert_element_type | solution.py:257
  615.6 12.1 %broadcast_select_fusion = f32[16,15,64,2,128]{4,3,2,1,0:T(2,128)} fusion(f32[16,15,64,2,128]{4,3,2,1,0:T(2,128)} %reshape.601, pred[16,15]{1,0:T(8,128)(4,1)S(1)} %compare_bitcast_fusion), kind=kLoop, calls=%fused_computation.5 | loop fusion | flops 3932160 | bytes 31457520 | tf_op jit(solution)/shard_map/jit(_where)/select_n | solution.py:259
  627.8 13.4 %copy.391 = f32[240,64,2,128]{3,1,2,0:T(8,128)} copy(f32[240,64,2,128]{3,2,1,0:T(2,128)} %bitcast.299) | data formatting | bytes 31457280 | tf_op jit(solution)/shard_map/jit(_where)/select_n | solution.py:259
  641.1 50.8 %scatter_fusion.1 = f32[10,64,2,4,128]{4,1,3,2,0:T(8,128)} fusion(f32[10,64,2,4,128]{4,1,3,2,0:T(8,128)} %copy.390, s32[240]{0:T(256)S(1)} %reshape.632, f32[240,64,2,128]{3,1,2,0:T(8,128)} %copy.391), kind=kCustom, calls=%fused_computation.4 | custom fusion | flops 3932160 | bytes 47187840 | tf_op jit(solution)/shard_map/scatter-add | solution.py:260
  696.3 3.7 convert_element_type.103
  700.0 5.4 reduce.20
  708.4 5.2 all-to-all-start.7
  718.4 3.7 convert_element_type.104
  722.1 5.4 reduce.21
  730.5 4.8 all-to-all-start.8
  735.3 5.0 broadcast_multiply_fusion
  (217 shorter events, 139.0 us)
Async XLA Ops:
  7.2 228.8 %copy-start = (bf16[512,2048]{1,0:T(8,128)(2,1)S(1)}, bf16[512,2048]{1,0:T(8,128)(2,1)}, u32[]{:S(2)}) copy-start(bf16[512,2048]{1,0:T(8,128)(2,1)} %param.22) | copy-start | bytes 6291460
  10.8 188.1 %copy-start.30 = (s32[160,1]{0,1:T(1,128)}, s32[160,1]{0,1:T(1,128)S(1)}, u32[]{:S(2)}) copy-start(s32[160,1]{0,1:T(1,128)S(1)} %compare_select_fusion.2) | copy-start | bytes 1924
  12.6 29.2 %all-to-all-start.3 = ((s32[16,1,15]{2,1,0:T(1,128)}), s32[16,1,15]{2,1,0:T(1,128)S(1)}, u32[]{:S(2)}, u32[]{:S(2)}) async-start(s32[16,1,15]{2,1,0:T(1,128)} %bitcast.20), calls=%async_computation.3 | async-start | bytes 16384 | tf_op jit(solution)/shard_map/all_to_all | solution.py:64
  41.8 25.3 %all-to-all-start.1 = ((bf16[4,2,40960]{2,1,0:T(2,128)(2,1)}), bf16[4,2,40960]{2,1,0:T(2,128)(2,1)}, u32[]{:S(2)}, u32[]{:S(2)}) async-start(bf16[4,2,40960]{2,1,0:T(2,128)(2,1)} %reshape.654), calls=%async_computation.1 | async-start | bytes 1310720 | tf_op jit(solution)/shard_map/all_to_all | solution.py:38
  67.2 35.8 %all-to-all-start = ((bf16[4,2,40960]{2,1,0:T(2,128)(2,1)}), bf16[4,2,40960]{2,1,0:T(2,128)(2,1)}, u32[]{:S(2)}, u32[]{:S(2)}) async-start(bf16[4,2,40960]{2,1,0:T(2,128)(2,1)} %reshape.656), calls=%async_computation | async-start | bytes 1310720 | tf_op jit(solution)/shard_map/all_to_all | solution.py:37
  71.9 164.0 %all-gather.4.cloned.1.call-start = ((), (), s32[]{:S(2)}) async-start(), calls=%async_computation.11 | async-start | bytes 3276800 | tf_op jit(solution)/shard_map/all_gather | solution.py:144
  103.0 17.0 %copy-start.20 = (bf16[1,4,160,512]{3,2,1,0:T(8,128)(2,1)}, bf16[1,4,160,512]{3,2,1,0:T(8,128)(2,1)S(1)}, u32[]{:S(2)}) copy-start(bf16[1,4,160,512]{3,2,1,0:T(8,128)(2,1)S(1)} %copy.320) | copy-start | bytes 1966084
  103.0 87.8 %all-to-all-start.2 = ((bf16[4,2,40960]{2,1,0:T(2,128)(2,1)}), bf16[4,2,40960]{2,1,0:T(2,128)(2,1)}, u32[]{:S(2)}, u32[]{:S(2)}) async-start(bf16[4,2,40960]{2,1,0:T(2,128)(2,1)} %reshape.658), calls=%async_computation.2 | async-start | bytes 1310720 | tf_op jit(solution)/shard_map/all_to_all | solution.py:36
  120.6 6.8 collective-permute-start
  124.0 9.0 %collective-permute-start.1 = (bf16[64,1024]{1,0:T(8,128)(2,1)S(1)}, bf16[64,1024]{1,0:T(8,128)(2,1)S(1)}, u32[]{:S(2)}, u32[]{:S(2)}) collective-permute-start(bf16[64,1024]{1,0:T(8,128)(2,1)S(1)} %get-tuple-element.80), channel_id=1, source_target_pairs={{4,0},{8,4},{12,8},{16,12},{20,16},{24,20},{28,24},{32,28},{36,32}... | collective-permute-start | bytes 393224 | tf_op jit(solution)/shard_map/ppermute | solution.py:20
  138.4 1.1 copy-start.8
  190.8 124.3 %all-to-all-start.4 = ((bf16[16,15,64,256]{3,2,1,0:T(8,128)(2,1)}), bf16[16,15,64,256]{3,2,1,0:T(8,128)(2,1)}, u32[]{:S(2)}, u32[]{:S(2)}) async-start(bf16[16,15,64,256]{3,2,1,0:T(8,128)(2,1)} %broadcast_select_fusion.1), calls=%async_computation.4 | async-start | bytes 15728640 | tf_op jit(solution)/shard_map/all_to_all | solution.py:72
  197.4 111.6 %all-gather.6.cloned.1.call-start = ((), (), s32[]{:S(2)}) async-start(), calls=%async_computation.14 | async-start | bytes 2228224 | tf_op jit(solution)/shard_map/all_gather | solution.py:9
  198.1 290.5 %all-reduce.5.cloned.1.call-start = ((), (), s32[]{:S(2)}) async-start(), calls=%async_computation.12 | async-start | bytes 524288 | tf_op jit(solution)/shard_map/psum | solution.py:229
  209.5 7.2 copy-start.9
  218.4 3.9 copy-start.21
  229.0 1.1 copy-start.10
  230.1 3.6 copy-start.6
  241.7 132.4 %copy-start.2 = (bf16[10,64,4,128]{3,2,1,0:T(4,128)(2,1)}, bf16[10,64,4,128]{3,2,1,0:T(4,128)(2,1)S(1)}, u32[]{:S(2)}) copy-start(bf16[10,64,4,128]{3,2,1,0:T(4,128)(2,1)S(1)} %reshape.592) | copy-start | bytes 1966084
  354.1 0.9 copy-start.29
  355.0 6.9 copy-start.1
  355.0 3.6 copy-start.13
  356.5 3.2 copy-start.5
  365.0 1.0 copy-start.28
  365.0 1.6 copy-start.27
  369.9 0.8 copy-start.25
  371.5 363.8 %all-reduce.7.cloned.1.call-start = ((), (), s32[]{:S(2)}) async-start(), calls=%async_computation.13 | async-start | bytes 8388608 | tf_op jit(solution)/shard_map/psum | solution.py:150
  374.1 3.2 copy-start.18
  374.1 3.2 copy-start.23
  381.2 4.0 slice-start
  381.2 4.1 slice-start.1
  384.6 1.3 copy-start.3
  384.6 2.1 copy-start.17
  386.7 3.2 copy-start.11
  388.4 1.5 copy-start.14
  396.2 5.1 copy-start.31
  454.1 7.8 %copy-start.19 = (bf16[10,64,4,128]{3,2,1,0:T(4,128)(2,1)S(1)}, bf16[10,64,4,128]{3,2,1,0:T(4,128)(2,1)}, u32[]{:S(2)}) copy-start(bf16[10,64,4,128]{3,2,1,0:T(4,128)(2,1)} %copy.351) | copy-start | bytes 1966084
  454.1 141.0 %all-to-all-start.6 = ((bf16[16,15,64,256]{3,2,1,0:T(8,128)(2,1)}), bf16[16,15,64,256]{3,2,1,0:T(8,128)(2,1)}, u32[]{:S(2)}, u32[]{:S(2)}) async-start(bf16[16,15,64,256]{3,2,1,0:T(8,128)(2,1)} %reshape.599), calls=%async_computation.7 | async-start | bytes 15728640 | tf_op jit(solution)/shard_map/all_to_all | solution.py:255
  461.4 286.1 %reduce-scatter.2.cloned.1.call-start = ((), (), s32[]{:S(2)}) async-start(), calls=%async_computation.10 | async-start | bytes 6553600 | tf_op jit(solution)/shard_map/reduce_scatter | solution.py:138
  465.7 1.1 copy-start.4
  466.8 2.8 copy-start.7
  469.7 2.9 copy-start.12
  472.6 1.1 copy-start.22
  474.5 2.2 copy-start.26
  474.7 3.5 copy-start.15
  474.8 4.2 copy-start.16
  492.8 71.6 %collective-permute-start.3 = (bf16[64,1024]{1,0:T(8,128)(2,1)S(1)}, bf16[64,1024]{1,0:T(8,128)(2,1)S(1)}, u32[]{:S(2)}, u32[]{:S(2)}) collective-permute-start(bf16[64,1024]{1,0:T(8,128)(2,1)S(1)} %concatenate.44), channel_id=1, source_target_pairs={{4,0},{8,4},{12,8},{16,12},{20,16},{24,20},{28,24},{32,28},{36,32}... | collective-permute-start | bytes 393224 | tf_op jit(solution)/shard_map/ppermute | solution.py:20
  495.7 89.1 %collective-permute-start.2 = (bf16[64,1024]{1,0:T(8,128)(2,1)S(1)}, bf16[64,1024]{1,0:T(8,128)(2,1)S(1)}, u32[]{:S(2)}, u32[]{:S(2)}) collective-permute-start(bf16[64,1024]{1,0:T(8,128)(2,1)S(1)} %concatenate.43), channel_id=1, source_target_pairs={{0,4},{4,8},{8,12},{12,16},{16,20},{20,24},{24,28},{28,32},{32,36}... | collective-permute-start | bytes 393224 | tf_op jit(solution)/shard_map/ppermute | solution.py:17
  595.1 113.3 %all-to-all-start.5 = ((bf16[4,2,40960]{2,1,0:T(2,128)(2,1)}), bf16[4,2,40960]{2,1,0:T(2,128)(2,1)}, u32[]{:S(2)}, u32[]{:S(2)}) async-start(bf16[4,2,40960]{2,1,0:T(2,128)(2,1)} %reshape.660), calls=%async_computation.6 | async-start | bytes 1310720 | tf_op jit(solution)/shard_map/all_to_all | solution.py:265
  708.4 22.1 %all-to-all-start.7 = ((bf16[4,2,40960]{2,1,0:T(2,128)(2,1)}), bf16[4,2,40960]{2,1,0:T(2,128)(2,1)}, u32[]{:S(2)}, u32[]{:S(2)}) async-start(bf16[4,2,40960]{2,1,0:T(2,128)(2,1)} %reshape.662), calls=%async_computation.8 | async-start | bytes 1310720 | tf_op jit(solution)/shard_map/all_to_all | solution.py:266
  715.9 1.1 copy-start.24
  730.5 13.7 %all-to-all-start.8 = ((bf16[4,2,40960]{2,1,0:T(2,128)(2,1)}), bf16[4,2,40960]{2,1,0:T(2,128)(2,1)}, u32[]{:S(2)}, u32[]{:S(2)}) async-start(bf16[4,2,40960]{2,1,0:T(2,128)(2,1)} %reshape.664), calls=%async_computation.9 | async-start | bytes 1310720 | tf_op jit(solution)/shard_map/all_to_all | solution.py:267
Sparse Core Ops, SparseCore 0:
  74.4 37.5 all-gather.3
  200.9 108.0 all-gather.5
  371.6 84.1 all-reduce.4
  459.6 197.9 all-reduce.6
  659.8 57.0 reduce-scatter.1
